TPU v7x, 512 devices: a whole 4x4x16 slice. The times are simulated.
512 devices in a mesh: gx: 16 (over z), gy: 8 (over y, x_lo), gz: 4 (over x_hi, core).
Axes of the slice: x: 4 (x_hi: 2, x_lo: 2; x = x_hi * 2 + x_lo), y: 4, z: 16, core: 2. Of those that a mesh axis runs over, the one named last changes fastest.
Arguments:
- velocity: float32 [3, 128, 64, 512], P(None, 'gx', 'gy', 'gz'), may hold values from -4 to 4
- sketch_prev: float32 [3, 64, 4, 32, 32, 128], P(None, 'gy', 'gz', 'gx'), may hold values from -6 to 6
- seed_matrix: int32 [512, 128], replicated, may hold values from -4 to 4
- snap_steps: int32 [4], replicated, may hold values from 0 to 511
- rank_keep: int32 [1], replicated, may hold values from 32 to 128
Outputs:
- velocity_out: float32 [3, 128, 64, 512], P(None, 'gx', 'gy', 'gz')
- mode_rows: float32 [3, 64, 4, 32, 32, 128], P(None, 'gy', 'gz', 'gx')
- factor: float32 [128, 128], replicated
All inputs are finite; a program needn't handle non-finite values.
Results may differ from a plain program's by a relative error of at most 0.0003.
Values sent between devices are 32-bit elements; how exact they have to be, the bound alone decides.
No kernel may reach another device: no remote copies, remote signals or barrier semaphores. Data moves between devices by JAX's collectives and lax.ppermute only.
A program may use at most 64 MiB of HBM per device.

v0:
```python
import math

import jax
import jax.numpy as jnp
from jax import lax
from jax.sharding import PartitionSpec as P

SNAPS = 4
STEPS = 2


TIME_STEP = 0.1
VISCOSITY = 0.4
ONE_THIRD = 1.0 / 3.0
TWO_THIRDS = 2.0 / 3.0
HIGHEST = lax.Precision.HIGHEST


def extended(block, sides, width):
    for axis, dim in sides:
        count = lax.axis_size(axis)
        forward = [(i, i + 1) for i in range(count - 1)]
        forward.append((count - 1, 0))
        backward = [(target, source) for source, target in forward]
        low = lax.ppermute(
            lax.slice_in_dim(block, block.shape[dim] - width, None, axis=dim), axis, forward
        )
        high = lax.ppermute(lax.slice_in_dim(block, 0, width, axis=dim), axis, backward)
        block = jnp.concatenate([low, block, high], axis=dim)
    return block


def tendency(padded):
    center = padded[:, 1:-1, 1:-1, 1:-1]
    forward = (padded[:, 2:, 1:-1, 1:-1], padded[:, 1:-1, 2:, 1:-1], padded[:, 1:-1, 1:-1, 2:])
    backward = (padded[:, :-2, 1:-1, 1:-1], padded[:, 1:-1, :-2, 1:-1], padded[:, 1:-1, 1:-1, :-2])
    convect = (
        center[0:1] * (forward[0] - backward[0])
        + center[1:2] * (forward[1] - backward[1])
        + center[2:3] * (forward[2] - backward[2])
    )
    spread = (
        forward[0]
        + backward[0]
        + forward[1]
        + backward[1]
        + forward[2]
        + backward[2]
        - 6.0 * center
    )
    return -0.5 * convect + VISCOSITY * spread


def with_walls(padded, margin):
    cells_y = padded.shape[2] - 2 * margin
    wall_rows = (
        lax.axis_index("gy") * cells_y - margin + jnp.arange(cells_y + 2 * margin, dtype=jnp.int32)
    )
    inside = ((wall_rows >= 0) & (wall_rows < lax.axis_size("gy") * cells_y)).astype(jnp.float32)
    return padded * inside[None, None, :, None]


def faces_padded(current):
    return with_walls(extended(current, (("gx", 1), ("gy", 2), ("gz", 3)), 1), 1)


def step_by_section(current):
    first_section = current + TIME_STEP * tendency(faces_padded(current))
    second_section = 0.75 * current + 0.25 * (
        first_section + TIME_STEP * tendency(faces_padded(first_section))
    )
    return ONE_THIRD * current + TWO_THIRDS * (
        second_section + TIME_STEP * tendency(faces_padded(second_section))
    )


def coarse_local(current):
    cells_x = current.shape[1]
    cells_y = current.shape[2]
    cells_z = current.shape[3]
    blocks = current.reshape(3, cells_x // 4, 4, cells_y, cells_z // 4, 4)
    return jnp.transpose(jnp.mean(blocks, axis=(2, 5)), (0, 2, 3, 1))


def on_device(velocity, sketch_prev, seed_matrix, snap_steps, rank_keep):
    current = velocity
    collected = []
    for snap_index in range(SNAPS):
        for step_index in range(STEPS):
            current = step_by_section(current)
        local_snap = coarse_local(current)
        collected.append(lax.all_to_all(local_snap, "gx", split_axis=2, concat_axis=3, tiled=True))
    stacked = jnp.stack(collected)
    rank_total = sketch_prev.shape[-1]
    snap_rows = stacked.reshape(stacked.shape[0], -1)
    picker = (
        snap_steps[:, None] == jnp.arange(seed_matrix.shape[0], dtype=jnp.int32)[None, :]
    ).astype(jnp.float32)
    omega_rows = 0.5 * jnp.dot(picker, seed_matrix.astype(jnp.float32), precision=HIGHEST)
    sketch_rows = sketch_prev.reshape(-1, rank_total) + lax.dot_general(
        snap_rows, omega_rows, (((0,), (0,)), ((), ())), precision=HIGHEST
    )
    local_gram = lax.dot_general(
        sketch_rows, sketch_rows, (((0,), (0,)), ((), ())), precision=HIGHEST
    )
    gram_sum = lax.psum(local_gram, ("gx", "gy", "gz"))
    lower_factor = jnp.linalg.cholesky(gram_sum)
    identity = jnp.eye(rank_total, dtype=jnp.float32)
    inverse = lax.linalg.triangular_solve(lower_factor, identity, left_side=True, lower=True).T
    total_rows = (
        sketch_rows.shape[0] * lax.axis_size("gx") * lax.axis_size("gy") * lax.axis_size("gz")
    )
    norm_scale = math.sqrt(total_rows)
    inside = (jnp.arange(rank_total, dtype=jnp.int32) < rank_keep[0]).astype(jnp.float32)
    mode_rows = norm_scale * jnp.dot(sketch_rows, inverse, precision=HIGHEST) * inside[None, :]
    factor = lower_factor.T * (1.0 / norm_scale) * inside[:, None] * inside[None, :]
    return (current, mode_rows.reshape(sketch_prev.shape), factor)


def solution(mesh):
    placed = (P(None, "gx", "gy", "gz"), P(None, "gy", "gz", "gx", None, None), P(), P(), P())
    return jax.shard_map(
        on_device,
        mesh=mesh,
        in_specs=placed,
        out_specs=(P(None, "gx", "gy", "gz"), P(None, "gy", "gz", "gx", None, None), P()),
        check_vma=False,
    )
```

profile of v0, /device:TPU:6, one launch (start us, length us, event | category | flops | bytes accessed | tf_op | source)
XLA Modules:
  0.0 1292.0 jit_solution(17506120628596611169)
XLA Ops:
  11.8 9.5 collective-permute-start.1
  28.6 4.4 collective-permute-done.3
  35.1 5.1 collective-permute-start.5
  46.6 5.4 collective-permute-start.7
  64.3 5.1 collective-permute-start.11
  75.8 5.4 collective-permute-start.13
  88.5 4.4 collective-permute-done.15
  95.0 5.1 collective-permute-start.17
  107.0 5.0 collective-permute-start.19
  124.2 5.1 collective-permute-start.23
  133.8 4.0 collective-permute-start.24
  149.3 4.1 collective-permute-done.27
  155.6 5.1 collective-permute-start.29
  165.2 5.3 collective-permute-start.30
  186.8 5.1 collective-permute-start.35
  196.4 3.9 collective-permute-start.36
  211.8 4.4 collective-permute-done.39
  218.3 5.1 collective-permute-start.41
  249.0 5.1 collective-permute-start.47
  279.1 5.1 collective-permute-start.53
  309.3 5.3 collective-permute-start.59
  322.1 4.0 collective-permute-start.61
  339.3 5.1 collective-permute-start.65
  369.9 5.1 collective-permute-start.71
  400.0 5.1 collective-permute-start.77
  430.2 5.1 collective-permute-start.83
  442.9 4.0 collective-permute-start.85
  460.2 5.1 collective-permute-start.89
  490.4 5.1 collective-permute-start.95
  520.5 5.1 collective-permute-start.101
  533.3 3.9 collective-permute-start.103
  550.6 5.1 collective-permute-start.107
  580.7 5.1 collective-permute-start.113
  611.4 5.1 collective-permute-start.119
  642.3 5.1 collective-permute-start.125
  673.2 5.1 collective-permute-start.131
  682.8 3.9 collective-permute-start.132
  704.2 5.1 collective-permute-start.137
  721.6 5.8 all-to-all-start
  740.2 5.1 collective-permute-start.143
  749.5 12.0 all-to-all-start.1
  762.8 12.2 all-to-all-done.1
  775.0 5.1 all-to-all-start.2
  780.8 13.2 %all-to-all-done.2 = f32[3,8,32,2]{1,3,0,2:T(2,128)S(1)} async-done(((f32[3,8,32,2]{1,3,0,2:T(2,128)}), f32[3,8,32,2]{1,3,0,2:T(2,128)S(1)}, u32[]{:S(2)}, u32[]{:S(2)}) %all-to-all-start.2) | async-done | bytes 6176 | tf_op jit(solution)/shard_map/all_to_all | solution.py:92
  800.7 10.3 all-to-all-done.3
  815.5 441.9 %all-reduce.2.cloned.1.call-done = f32[128,128]{0,1:T(8,128)} async-done(((f32[128,128]{0,1:T(8,128)}), f32[128,128]{0,1:T(8,128)}) %all-reduce.2.cloned.1.call-update) | async-done | bytes 65552 | tf_op jit(solution)/shard_map/psum | solution.py:106
  1259.1 11.7 cholesky.17
  1273.0 9.8 custom-call.6
  (477 shorter events, 556.5 us)
Async XLA Ops:
  8.0 13.3 %collective-permute-start = (f32[3,1,8,128]{3,2,1,0:T(8,128)S(1)}, f32[3,1,8,128]{3,2,1,0:T(8,128)S(1)}, u32[]{:S(2)}, u32[]{:S(2)}) collective-permute-start(f32[3,1,8,128]{3,2,1,0:T(8,128)S(1)} %get-tuple-element.230), channel_id=1, source_target_pairs={{0,32},{32,64},{64,96},{96,128},{128,160},{160,192},{192,224},{224... | collective-permute-start | bytes 36872 | tf_op jit(solution)/shard_map/ppermute | solution.py:25
  11.8 10.9 collective-permute-start.1
  33.1 9.0 collective-permute-start.4
  35.1 8.8 collective-permute-start.5
  62.4 9.0 collective-permute-start.10
  64.3 8.8 collective-permute-start.11
  93.1 9.0 collective-permute-start.16
  95.0 8.8 collective-permute-start.17
  122.3 9.0 collective-permute-start.22
  124.2 8.8 collective-permute-start.23
  153.7 9.0 collective-permute-start.28
  155.6 8.8 collective-permute-start.29
  184.8 9.0 collective-permute-start.34
  186.8 8.8 collective-permute-start.35
  216.4 9.0 collective-permute-start.40
  218.3 8.8 collective-permute-start.41
  247.1 9.0 collective-permute-start.46
  277.2 9.0 collective-permute-start.52
  307.4 9.0 collective-permute-start.58
  309.3 8.8 collective-permute-start.59
  337.4 9.0 collective-permute-start.64
  367.9 9.0 collective-permute-start.70
  369.9 8.8 collective-permute-start.71
  398.1 9.0 collective-permute-start.76
  428.3 9.0 collective-permute-start.82
  458.3 9.0 collective-permute-start.88
  460.2 8.8 collective-permute-start.89
  488.4 9.0 collective-permute-start.94
  490.4 8.8 collective-permute-start.95
  518.5 9.0 collective-permute-start.100
  520.5 8.8 collective-permute-start.101
  548.7 9.0 collective-permute-start.106
  550.6 8.8 collective-permute-start.107
  578.8 9.0 collective-permute-start.112
  580.7 8.8 collective-permute-start.113
  609.5 9.0 collective-permute-start.118
  640.4 9.0 collective-permute-start.124
  671.3 9.0 collective-permute-start.130
  702.2 9.0 collective-permute-start.136
  704.2 8.8 collective-permute-start.137
  713.8 14.5 %collective-permute-start.138 = (f32[3,1,8,128]{3,2,1,0:T(8,128)S(1)}, f32[3,1,8,128]{3,2,1,0:T(8,128)S(1)}, u32[]{:S(2)}, u32[]{:S(2)}) collective-permute-start(f32[3,1,8,128]{3,2,1,0:T(8,128)S(1)} %get-tuple-element.183), channel_id=1, source_target_pairs={{0,32},{32,64},{64,96},{96,128},{128,160},{160,192},{192,224},{224... | collective-permute-start | bytes 36872 | tf_op jit(solution)/shard_map/ppermute | solution.py:25
  717.5 10.8 collective-permute-start.139
  721.6 28.0 %all-to-all-start = ((f32[3,8,32,2]{1,3,0,2:T(2,128)}), f32[3,8,32,2]{1,3,0,2:T(2,128)S(1)}, u32[]{:S(2)}, u32[]{:S(2)}) async-start(f32[3,8,32,2]{1,3,0,2:T(2,128)} %copy.41), calls=%async_computation | async-start | bytes 196608 | tf_op jit(solution)/shard_map/all_to_all | solution.py:92
  738.2 9.0 collective-permute-start.142
  749.5 25.5 %all-to-all-start.1 = ((f32[3,8,32,2]{1,3,0,2:T(2,128)}), f32[3,8,32,2]{1,3,0,2:T(2,128)S(1)}, u32[]{:S(2)}, u32[]{:S(2)}) async-start(f32[3,8,32,2]{1,3,0,2:T(2,128)} %copy.45), calls=%async_computation.1 | async-start | bytes 196608 | tf_op jit(solution)/shard_map/all_to_all | solution.py:92
  775.0 19.1 %all-to-all-start.2 = ((f32[3,8,32,2]{1,3,0,2:T(2,128)}), f32[3,8,32,2]{1,3,0,2:T(2,128)S(1)}, u32[]{:S(2)}, u32[]{:S(2)}) async-start(f32[3,8,32,2]{1,3,0,2:T(2,128)} %copy.49), calls=%async_computation.2 | async-start | bytes 196608 | tf_op jit(solution)/shard_map/all_to_all | solution.py:92
  794.1 16.9 %all-to-all-start.3 = ((f32[3,8,32,2]{1,3,0,2:T(2,128)}), f32[3,8,32,2]{1,3,0,2:T(2,128)S(1)}, u32[]{:S(2)}, u32[]{:S(2)}) async-start(f32[3,8,32,2]{1,3,0,2:T(2,128)} %copy.53), calls=%async_computation.3 | async-start | bytes 196608 | tf_op jit(solution)/shard_map/all_to_all | solution.py:92
  797.6 459.8 %all-reduce.2.cloned.1.call-start = ((), (), s32[]{:S(2)}) async-start(), calls=%async_computation.4 | async-start | bytes 131072 | tf_op jit(solution)/shard_map/psum | solution.py:106
  (106 other events, 768.8 us)
Sparse Core Ops, SparseCore 0:
  815.6 441.7 all-reduce.1
where the time goes:
time: 1310 us; the launch traced here: 1290 us
  waiting for transfers between devices  695 us (53%)
  starting transfers between devices  514 us (39%)
  other arithmetic  42.5 us (3%)
  between operations  18.1 us (1%)
  local copies, waits for them, and re-layouts  17.1 us (1%)
    psum x1, waiting for transfers between devices, on_device(): gram_sum = lax.psum(local_gram, ('gx', 'gy', 'gz'))  442 us
    ppermute x72, starting transfers between devices, extended(): lax.ppermute(lax.slice_in_dim(block, 0, width, axis=dim), axis, backward)  286 us
    ppermute x72, starting transfers between devices, extended(): lax.ppermute(lax.slice_in_dim(block, block.shape[dim] - width, None, axis...  201 us
    ppermute x72, waiting for transfers between devices, extended(): lax.ppermute(lax.slice_in_dim(block, 0, width, axis=dim), axis, backward)  172 us
    ppermute x72, waiting for transfers between devices, extended(): lax.ppermute(lax.slice_in_dim(block, block.shape[dim] - width, None, axis...  44.7 us
    all_to_all x4, waiting for transfers between devices, on_device(): lax.all_to_all(local_snap, 'gx', split_axis=2, concat_axis=3, tiled=True)  35.7 us
    all_to_all x4, starting transfers between devices, on_device(): lax.all_to_all(local_snap, 'gx', split_axis=2, concat_axis=3, tiled=True)  26.4 us
  transfers between devices with their start and end apart: 149, of which 99 were waited for; matrix products, arithmetic and copies ran while one was open for 1% of the time, Pallas kernels for 0%

commit v1 on v0

--- a/solution.py
+++ b/solution.py
@@ -7,6 +7,7 @@
 
 SNAPS = 4
 STEPS = 2
+HALO = 3 * STEPS
 
 
 TIME_STEP = 0.1
@@ -19,8 +20,7 @@
 def extended(block, sides, width):
     for axis, dim in sides:
         count = lax.axis_size(axis)
-        forward = [(i, i + 1) for i in range(count - 1)]
-        forward.append((count - 1, 0))
+        forward = [(i, (i + 1) % count) for i in range(count)]
         backward = [(target, source) for source, target in forward]
         low = lax.ppermute(
             lax.slice_in_dim(block, block.shape[dim] - width, None, axis=dim), axis, forward
@@ -51,26 +51,35 @@
     return -0.5 * convect + VISCOSITY * spread
 
 
-def with_walls(padded, margin):
-    cells_y = padded.shape[2] - 2 * margin
-    wall_rows = (
-        lax.axis_index("gy") * cells_y - margin + jnp.arange(cells_y + 2 * margin, dtype=jnp.int32)
-    )
-    inside = ((wall_rows >= 0) & (wall_rows < lax.axis_size("gy") * cells_y)).astype(jnp.float32)
-    return padded * inside[None, None, :, None]
+def trim(block, width):
+    return block[:, width:-width, width:-width, width:-width]
 
 
-def faces_padded(current):
-    return with_walls(extended(current, (("gx", 1), ("gy", 2), ("gz", 3)), 1), 1)
+def wall_mask(cells_y, margin):
+    rows = lax.axis_index("gy") * cells_y - margin + jnp.arange(cells_y + 2 * margin, dtype=jnp.int32)
+    inside = ((rows >= 0) & (rows < lax.axis_size("gy") * cells_y)).astype(jnp.float32)
+    return inside[None, None, :, None]
 
 
-def step_by_section(current):
-    first_section = current + TIME_STEP * tendency(faces_padded(current))
-    second_section = 0.75 * current + 0.25 * (
-        first_section + TIME_STEP * tendency(faces_padded(first_section))
+def walled(block, cells_y, margin):
+    if margin == 0:
+        return block
+    return block * wall_mask(cells_y, margin)
+
+
+def step_shrinking(current, cells_y, margin):
+    first_section = walled(trim(current, 1) + TIME_STEP * tendency(current), cells_y, margin - 1)
+    second_section = walled(
+        0.75 * trim(current, 2)
+        + 0.25 * (trim(first_section, 1) + TIME_STEP * tendency(first_section)),
+        cells_y,
+        margin - 2,
     )
-    return ONE_THIRD * current + TWO_THIRDS * (
-        second_section + TIME_STEP * tendency(faces_padded(second_section))
+    return walled(
+        ONE_THIRD * trim(current, 3)
+        + TWO_THIRDS * (trim(second_section, 1) + TIME_STEP * tendency(second_section)),
+        cells_y,
+        margin - 3,
     )
 
 
@@ -82,15 +91,28 @@
     return jnp.transpose(jnp.mean(blocks, axis=(2, 5)), (0, 2, 3, 1))
 
 
+def butterfly_sum(value, axes):
+    for axis in axes:
+        count = lax.axis_size(axis)
+        bit = 1
+        while bit < count:
+            value = value + lax.ppermute(value, axis, [(i, i ^ bit) for i in range(count)])
+            bit *= 2
+    return value
+
+
 def on_device(velocity, sketch_prev, seed_matrix, snap_steps, rank_keep):
     current = velocity
+    cells_y = current.shape[2]
     collected = []
     for snap_index in range(SNAPS):
+        margin = HALO
+        current = walled(extended(current, (("gx", 1), ("gy", 2), ("gz", 3)), HALO), cells_y, margin)
         for step_index in range(STEPS):
-            current = step_by_section(current)
-        local_snap = coarse_local(current)
-        collected.append(lax.all_to_all(local_snap, "gx", split_axis=2, concat_axis=3, tiled=True))
-    stacked = jnp.stack(collected)
+            current = step_shrinking(current, cells_y, margin)
+            margin -= 3
+        collected.append(coarse_local(current))
+    stacked = lax.all_to_all(jnp.stack(collected), "gx", split_axis=3, concat_axis=4, tiled=True)
     rank_total = sketch_prev.shape[-1]
     snap_rows = stacked.reshape(stacked.shape[0], -1)
     picker = (
@@ -103,7 +125,7 @@
     local_gram = lax.dot_general(
         sketch_rows, sketch_rows, (((0,), (0,)), ((), ())), precision=HIGHEST
     )
-    gram_sum = lax.psum(local_gram, ("gx", "gy", "gz"))
+    gram_sum = butterfly_sum(local_gram, ("gz", "gy", "gx"))
     lower_factor = jnp.linalg.cholesky(gram_sum)
     identity = jnp.eye(rank_total, dtype=jnp.float32)
     inverse = lax.linalg.triangular_solve(lower_factor, identity, left_side=True, lower=True).T

time: 1310 us -> 381 us (0.29)
  waiting for transfers between devices: 695 us -> 69.7 us
  starting transfers between devices: 514 us -> 127 us
  local copies, waits for them, and re-layouts: 17.1 us -> 82.7 us
  other arithmetic: 42.5 us -> 87.8 us
  between operations: 18.1 us -> 2.68 us
    psum x1 -> x0, waiting for transfers between devices: 442 us -> none  [on_device(): gram_sum = lax.psum(local_gram, ('gx', 'gy', 'gz'))]
    ppermute x72 -> x12, starting transfers between devices: 286 us -> 55.3 us  [extended(): lax.ppermute(lax.slice_in_dim(block, 0, width, axis=dim), axis, backward)]
    ppermute x72 -> x12, starting transfers between devices: 201 us -> 34.6 us  [extended(): lax.ppermute(lax.slice_in_dim(block, block.shape[dim] - width, None, axis...]
    ppermute x72 -> x12, waiting for transfers between devices: 172 us -> 9.26 us  [extended(): lax.ppermute(lax.slice_in_dim(block, 0, width, axis=dim), axis, backward)]
    ppermute x0 -> x9, waiting for transfers between devices: none -> 45.3 us  [butterfly_sum(): lax.ppermute(value, axis, [(i, i ^ bit) for i in range(count)])]
    ppermute x72 -> x12, waiting for transfers between devices: 44.7 us -> 2.6 us  [extended(): lax.ppermute(lax.slice_in_dim(block, block.shape[dim] - width, None, axis...]
    ppermute x0 -> x16, local copies, waits for them, and re-layouts: none -> 30.7 us  [the longest x8 15.4 us: extended(): lax.ppermute(lax.slice_in_dim(block, 0, width, axis=dim), axis, backward)]
    concatenate x24 -> x7, other arithmetic: 1.21 us -> 30.5 us  [extended(): block = jnp.concatenate([low, block, high], axis=dim)]
  transfers between devices with their start and end apart: 149 -> 34, of which waited for: 99 -> 23; matrix products, arithmetic and copies ran while one was open for 1% -> 13% of each run, Pallas kernels for 0% -> 0%
where the time goes in v1:
time: 381 us; the launch traced here: 374 us
  starting transfers between devices  127 us (33%)
  other arithmetic  87.8 us (23%)
  local copies, waits for them, and re-layouts  82.7 us (22%)
  waiting for transfers between devices  69.7 us (18%)
  matrix products  4.29 us (1%)
    ppermute x12, starting transfers between devices, extended(): lax.ppermute(lax.slice_in_dim(block, 0, width, axis=dim), axis, backward)  55.3 us
    ppermute x9, waiting for transfers between devices, butterfly_sum(): lax.ppermute(value, axis, [(i, i ^ bit) for i in range(count)])  45.3 us
    ppermute x12, starting transfers between devices, extended(): lax.ppermute(lax.slice_in_dim(block, block.shape[dim] - width, None, axis...  34.6 us
    mul x24, other arithmetic, walled(): return block * wall_mask(cells_y, margin)  30.5 us
    concatenate x7, other arithmetic, extended(): block = jnp.concatenate([low, block, high], axis=dim)  30.5 us
    concatenate x9, local copies, waits for them, and re-layouts, extended(): block = jnp.concatenate([low, block, high], axis=dim)  28.2 us
    ppermute x9, starting transfers between devices, butterfly_sum(): lax.ppermute(value, axis, [(i, i ^ bit) for i in range(count)])  26.9 us
    ppermute x8, local copies, waits for them, and re-layouts, extended(): lax.ppermute(lax.slice_in_dim(block, 0, width, axis=dim), axis, backward)  15.4 us
  transfers between devices with their start and end apart: 34, of which 23 were waited for; matrix products, arithmetic and copies ran while one was open for 13% of the time, Pallas kernels for 0%

profile of v1, /device:TPU:6, one launch (start us, length us, event | category | flops | bytes accessed | tf_op | source)
XLA Modules:
  0.0 373.8 jit_solution(6173954067066277898)
XLA Ops:
  1.6 3.8 %collective-permute-start = (f32[3,6,8,128]{3,2,1,0:T(8,128)S(1)}, f32[3,6,8,128]{3,2,1,0:T(8,128)S(1)}, u32[]{:S(2)}, u32[]{:S(2)}) collective-permute-start(f32[3,6,8,128]{3,2,1,0:T(8,128)S(1)} %get-tuple-element.113), channel_id=1, source_target_pairs={{0,32},{32,64},{64,96},{96,128},{128,160},{160,192},{192,224},{224... | collective-permute-start | bytes 221192 | tf_op jit(solution)/shard_map/ppermute | solution.py:25
  5.4 9.5 %collective-permute-start.1 = (f32[3,6,8,128]{3,2,1,0:T(8,128)S(1)}, f32[3,6,8,128]{3,2,1,0:T(8,128)S(1)}, u32[]{:S(2)}, u32[]{:S(2)}) collective-permute-start(f32[3,6,8,128]{3,2,1,0:T(8,128)S(1)} %get-tuple-element.112), channel_id=1, source_target_pairs={{32,0},{64,32},{96,64},{128,96},{160,128},{192,160},{224,192},{256... | collective-permute-start | bytes 221192 | tf_op jit(solution)/shard_map/ppermute | solution.py:28
  17.0 3.8 %collective-permute-start.2 = (f32[3,20,6,128]{3,1,2,0:T(8,128)S(1)}, f32[3,20,6,128]{3,1,2,0:T(8,128)S(1)}, u32[]{:S(2)}, u32[]{:S(2)}) collective-permute-start(f32[3,20,6,128]{3,1,2,0:T(8,128)S(1)} %copy.132), channel_id=1, source_target_pairs={{0,4},{4,8},{8,12},{12,16},{16,20},{20,24},{24,28},{28,0},{1,5},{5... | collective-permute-start | bytes 552968 | tf_op jit(solution)/shard_map/ppermute | solution.py:25
  22.9 3.4 copy.90
  26.6 3.3 copy.89
  31.0 3.4 copy.91
  34.3 7.6 %pad_maximum_fusion = f32[3,20,20,128]{2,1,3,0:T(8,128)S(1)} fusion(f32[3,20,6,128]{2,1,3,0:T(8,128)} %copy.91, f32[3,20,8,128]{2,1,3,0:T(8,128)} %copy.90, f32[3,20,6,128]{2,1,3,0:T(8,128)} %copy.89), kind=kLoop, calls=%fused_computation | loop fusion | flops 307200 | bytes 1228800 | tf_op jit(solution)/shard_map/concatenate | solution.py:29
  46.1 5.6 %collective-permute-start.5 = (f32[3,20,20,6]{2,1,3,0:T(8,128)S(1)}, f32[3,20,20,6]{2,1,3,0:T(8,128)S(1)}, u32[]{:S(2)}, u32[]{:S(2)}) collective-permute-start(f32[3,20,20,6]{2,1,3,0:T(8,128)S(1)} %get-tuple-element.25), channel_id=1, source_target_pairs={{1,0},{2,1},{3,2},{0,3},{5,4},{6,5},{7,6},{4,7},{9,8},{10,9},{11,1... | collective-permute-start | bytes 86408 | tf_op jit(solution)/shard_map/ppermute | solution.py:28
  51.7 3.7 copy.93
  67.7 5.2 %collective-permute-start.7 = (f32[3,6,8,128]{3,2,1,0:T(8,128)S(1)}, f32[3,6,8,128]{3,2,1,0:T(8,128)S(1)}, u32[]{:S(2)}, u32[]{:S(2)}) collective-permute-start(f32[3,6,8,128]{3,2,1,0:T(8,128)S(1)} %get-tuple-element.111), channel_id=1, source_target_pairs={{32,0},{64,32},{96,64},{128,96},{160,128},{192,160},{224,192},{256... | collective-permute-start | bytes 221192 | tf_op jit(solution)/shard_map/ppermute | solution.py:28
  75.2 4.4 %collective-permute-start.8 = (f32[3,20,6,128]{3,1,2,0:T(8,128)S(1)}, f32[3,20,6,128]{3,1,2,0:T(8,128)S(1)}, u32[]{:S(2)}, u32[]{:S(2)}) collective-permute-start(f32[3,20,6,128]{3,1,2,0:T(8,128)S(1)} %copy.134), channel_id=1, source_target_pairs={{0,4},{4,8},{8,12},{12,16},{16,20},{20,24},{24,28},{28,0},{1,5},{5... | collective-permute-start | bytes 552968 | tf_op jit(solution)/shard_map/ppermute | solution.py:25
  81.7 3.4 copy.98
  85.3 3.3 copy.97
  89.7 3.4 copy.99
  93.1 7.6 %pad_maximum_fusion.1 = f32[3,20,20,128]{2,1,3,0:T(8,128)S(1)} fusion(f32[3,20,6,128]{2,1,3,0:T(8,128)} %copy.99, f32[3,20,8,128]{2,1,3,0:T(8,128)} %copy.98, f32[3,20,6,128]{2,1,3,0:T(8,128)} %copy.97), kind=kLoop, calls=%fused_computation.1 | loop fusion | flops 307200 | bytes 1228800 | tf_op jit(solution)/shard_map/concatenate | solution.py:29
  104.8 5.1 %collective-permute-start.11 = (f32[3,20,20,6]{2,1,3,0:T(8,128)S(1)}, f32[3,20,20,6]{2,1,3,0:T(8,128)S(1)}, u32[]{:S(2)}, u32[]{:S(2)}) collective-permute-start(f32[3,20,20,6]{2,1,3,0:T(8,128)S(1)} %get-tuple-element.23), channel_id=1, source_target_pairs={{1,0},{2,1},{3,2},{0,3},{5,4},{6,5},{7,6},{4,7},{9,8},{10,9},{11,1... | collective-permute-start | bytes 86408 | tf_op jit(solution)/shard_map/ppermute | solution.py:28
  110.0 3.7 copy.101
  126.0 5.6 %collective-permute-start.13 = (f32[3,6,8,128]{3,2,1,0:T(8,128)S(1)}, f32[3,6,8,128]{3,2,1,0:T(8,128)S(1)}, u32[]{:S(2)}, u32[]{:S(2)}) collective-permute-start(f32[3,6,8,128]{3,2,1,0:T(8,128)S(1)} %get-tuple-element.109), channel_id=1, source_target_pairs={{32,0},{64,32},{96,64},{128,96},{160,128},{192,160},{224,192},{256... | collective-permute-start | bytes 221192 | tf_op jit(solution)/shard_map/ppermute | solution.py:28
  133.7 4.2 %collective-permute-start.14 = (f32[3,20,6,128]{3,1,2,0:T(8,128)S(1)}, f32[3,20,6,128]{3,1,2,0:T(8,128)S(1)}, u32[]{:S(2)}, u32[]{:S(2)}) collective-permute-start(f32[3,20,6,128]{3,1,2,0:T(8,128)S(1)} %copy.136), channel_id=1, source_target_pairs={{0,4},{4,8},{8,12},{12,16},{16,20},{20,24},{24,28},{28,0},{1,5},{5... | collective-permute-start | bytes 552968 | tf_op jit(solution)/shard_map/ppermute | solution.py:25
  140.5 3.4 copy.106
  143.9 3.3 copy.105
  149.3 3.4 copy.107
  152.7 7.6 %pad_maximum_fusion.2 = f32[3,20,20,128]{2,1,3,0:T(8,128)S(1)} fusion(f32[3,20,6,128]{2,1,3,0:T(8,128)} %copy.107, f32[3,20,8,128]{2,1,3,0:T(8,128)} %copy.106, f32[3,20,6,128]{2,1,3,0:T(8,128)} %copy.105), kind=kLoop, calls=%fused_computation.2 | loop fusion | flops 307200 | bytes 1228800 | tf_op jit(solution)/shard_map/concatenate | solution.py:29
  164.6 5.0 %collective-permute-start.17 = (f32[3,20,20,6]{2,1,3,0:T(8,128)S(1)}, f32[3,20,20,6]{2,1,3,0:T(8,128)S(1)}, u32[]{:S(2)}, u32[]{:S(2)}) collective-permute-start(f32[3,20,20,6]{2,1,3,0:T(8,128)S(1)} %get-tuple-element.21), channel_id=1, source_target_pairs={{1,0},{2,1},{3,2},{0,3},{5,4},{6,5},{7,6},{4,7},{9,8},{10,9},{11,1... | collective-permute-start | bytes 86408 | tf_op jit(solution)/shard_map/ppermute | solution.py:28
  169.6 3.7 copy.109
  185.7 5.2 %collective-permute-start.19 = (f32[3,6,8,128]{3,2,1,0:T(8,128)S(1)}, f32[3,6,8,128]{3,2,1,0:T(8,128)S(1)}, u32[]{:S(2)}, u32[]{:S(2)}) collective-permute-start(f32[3,6,8,128]{3,2,1,0:T(8,128)S(1)} %get-tuple-element.107), channel_id=1, source_target_pairs={{32,0},{64,32},{96,64},{128,96},{160,128},{192,160},{224,192},{256... | collective-permute-start | bytes 221192 | tf_op jit(solution)/shard_map/ppermute | solution.py:28
  193.0 4.8 %collective-permute-start.20 = (f32[3,20,6,128]{3,1,2,0:T(8,128)S(1)}, f32[3,20,6,128]{3,1,2,0:T(8,128)S(1)}, u32[]{:S(2)}, u32[]{:S(2)}) collective-permute-start(f32[3,20,6,128]{3,1,2,0:T(8,128)S(1)} %copy.138), channel_id=1, source_target_pairs={{0,4},{4,8},{8,12},{12,16},{16,20},{20,24},{24,28},{28,0},{1,5},{5... | collective-permute-start | bytes 552968 | tf_op jit(solution)/shard_map/ppermute | solution.py:25
  201.9 3.4 copy.114
  205.3 3.3 copy.113
  208.6 3.4 copy.115
  212.0 7.6 %pad_maximum_fusion.3 = f32[3,20,20,128]{2,1,3,0:T(8,128)S(1)} fusion(f32[3,20,6,128]{2,1,3,0:T(8,128)} %copy.115, f32[3,20,8,128]{2,1,3,0:T(8,128)} %copy.114, f32[3,20,6,128]{2,1,3,0:T(8,128)} %copy.113), kind=kLoop, calls=%fused_computation.3 | loop fusion | flops 307200 | bytes 1228800 | tf_op jit(solution)/shard_map/concatenate | solution.py:29
  223.7 5.1 %collective-permute-start.23 = (f32[3,20,20,6]{2,1,3,0:T(8,128)S(1)}, f32[3,20,20,6]{2,1,3,0:T(8,128)S(1)}, u32[]{:S(2)}, u32[]{:S(2)}) collective-permute-start(f32[3,20,20,6]{2,1,3,0:T(8,128)S(1)} %get-tuple-element.19), channel_id=1, source_target_pairs={{1,0},{2,1},{3,2},{0,3},{5,4},{6,5},{7,6},{4,7},{9,8},{10,9},{11,1... | collective-permute-start | bytes 86408 | tf_op jit(solution)/shard_map/ppermute | solution.py:28
  229.9 3.7 copy.117
  246.5 9.9 %all-to-all-start = ((f32[16,1,384]{2,1,0:T(1,128)}), f32[16,1,384]{2,1,0:T(1,128)S(1)}, u32[]{:S(2)}, u32[]{:S(2)}) async-start(f32[16,1,384]{2,1,0:T(1,128)} %reshape.103), calls=%async_computation | async-start | bytes 49152 | tf_op jit(solution)/shard_map/all_to_all | solution.py:115
  256.7 12.5 %all-to-all-done = f32[16,1,384]{2,1,0:T(1,128)S(1)} async-done(((f32[16,1,384]{2,1,0:T(1,128)}), f32[16,1,384]{2,1,0:T(1,128)S(1)}, u32[]{:S(2)}, u32[]{:S(2)}) %all-to-all-start) | async-done | bytes 24608 | tf_op jit(solution)/shard_map/all_to_all | solution.py:115
  278.0 3.9 %collective-permute-start.25 = (f32[128,128]{0,1:T(8,128)S(1)}, f32[128,128]{0,1:T(8,128)S(1)}, u32[]{:S(2)}, u32[]{:S(2)}) collective-permute-start(f32[128,128]{0,1:T(8,128)S(1)} %add.1084), channel_id=1, source_target_pairs={{0,2},{1,3},{2,0},{3,1},{4,6},{5,7},{6,4},{7,5},{8,10},{9,11},{10,... | collective-permute-start | bytes 196616 | tf_op jit(solution)/shard_map/ppermute | solution.py:99
  282.0 3.7 collective-permute-done.25
  285.7 5.8 %collective-permute-start.26 = (f32[128,128]{0,1:T(8,128)S(1)}, f32[128,128]{0,1:T(8,128)S(1)}, u32[]{:S(2)}, u32[]{:S(2)}) collective-permute-start(f32[128,128]{0,1:T(8,128)S(1)} %add.1085), channel_id=1, source_target_pairs={{0,4},{4,0},{8,12},{12,8},{16,20},{20,16},{24,28},{28,24},{1,5},{5... | collective-permute-start | bytes 196616 | tf_op jit(solution)/shard_map/ppermute | solution.py:99
  295.7 4.2 %collective-permute-done.27 = f32[128,128]{0,1:T(8,128)S(1)} collective-permute-done((f32[128,128]{0,1:T(8,128)S(1)}, f32[128,128]{0,1:T(8,128)S(1)}, u32[]{:S(2)}, u32[]{:S(2)}) %collective-permute-start.27) | collective-permute-done | bytes 65568 | tf_op jit(solution)/shard_map/ppermute | solution.py:99
  302.5 5.1 %collective-permute-done.28 = f32[128,128]{0,1:T(8,128)S(1)} collective-permute-done((f32[128,128]{0,1:T(8,128)S(1)}, f32[128,128]{0,1:T(8,128)S(1)}, u32[]{:S(2)}, u32[]{:S(2)}) %collective-permute-start.28) | collective-permute-done | bytes 65568 | tf_op jit(solution)/shard_map/ppermute | solution.py:99
  307.6 2.7 collective-permute-start.29
  310.3 3.5 collective-permute-done.29
  316.9 3.9 %collective-permute-done.30 = f32[128,128]{0,1:T(8,128)S(1)} collective-permute-done((f32[128,128]{0,1:T(8,128)S(1)}, f32[128,128]{0,1:T(8,128)S(1)}, u32[]{:S(2)}, u32[]{:S(2)}) %collective-permute-start.30) | collective-permute-done | bytes 65568 | tf_op jit(solution)/shard_map/ppermute | solution.py:99
  323.5 8.9 %collective-permute-done.31 = f32[128,128]{0,1:T(8,128)S(1)} collective-permute-done((f32[128,128]{0,1:T(8,128)S(1)}, f32[128,128]{0,1:T(8,128)S(1)}, u32[]{:S(2)}, u32[]{:S(2)}) %collective-permute-start.31) | collective-permute-done | bytes 65568 | tf_op jit(solution)/shard_map/ppermute | solution.py:99
  332.4 2.9 collective-permute-start.32
  335.4 12.5 %collective-permute-done.32 = f32[128,128]{0,1:T(8,128)S(1)} collective-permute-done((f32[128,128]{0,1:T(8,128)S(1)}, f32[128,128]{0,1:T(8,128)S(1)}, u32[]{:S(2)}, u32[]{:S(2)}) %collective-permute-start.32) | collective-permute-done | bytes 65568 | tf_op jit(solution)/shard_map/ppermute | solution.py:99
  348.0 11.7 %cholesky.17 = f32[128,128]{1,0:T(8,128)S(1)} custom-call(f32[128,128]{1,0:T(8,128)S(1)} %fusion.31), custom_call_target="Cholesky" | custom-call | tf_op jit(solution)/shard_map/jit(cholesky)/cholesky | solution.py:129
  361.1 9.8 %custom-call.6 = f32[1,128,128]{1,2,0:T(8,128)S(1)} custom-call(f32[1,128,128]{2,1,0:T(8,128)S(1)} %get-tuple-element.115), custom_call_target="InvertDiagBlocksLowerTriangular" | custom-call | tf_op jit(solution)/shard_map/triangular_solve | solution.py:131
  (190 shorter events, 117.2 us)
Async XLA Ops:
  1.6 13.7 %collective-permute-start = (f32[3,6,8,128]{3,2,1,0:T(8,128)S(1)}, f32[3,6,8,128]{3,2,1,0:T(8,128)S(1)}, u32[]{:S(2)}, u32[]{:S(2)}) collective-permute-start(f32[3,6,8,128]{3,2,1,0:T(8,128)S(1)} %get-tuple-element.113), channel_id=1, source_target_pairs={{0,32},{32,64},{64,96},{96,128},{128,160},{160,192},{192,224},{224... | collective-permute-start | bytes 221192 | tf_op jit(solution)/shard_map/ppermute | solution.py:25
  5.4 11.5 %collective-permute-start.1 = (f32[3,6,8,128]{3,2,1,0:T(8,128)S(1)}, f32[3,6,8,128]{3,2,1,0:T(8,128)S(1)}, u32[]{:S(2)}, u32[]{:S(2)}) collective-permute-start(f32[3,6,8,128]{3,2,1,0:T(8,128)S(1)} %get-tuple-element.112), channel_id=1, source_target_pairs={{32,0},{64,32},{96,64},{128,96},{160,128},{192,160},{224,192},{256... | collective-permute-start | bytes 221192 | tf_op jit(solution)/shard_map/ppermute | solution.py:28
  17.0 9.6 %collective-permute-start.2 = (f32[3,20,6,128]{3,1,2,0:T(8,128)S(1)}, f32[3,20,6,128]{3,1,2,0:T(8,128)S(1)}, u32[]{:S(2)}, u32[]{:S(2)}) collective-permute-start(f32[3,20,6,128]{3,1,2,0:T(8,128)S(1)} %copy.132), channel_id=1, source_target_pairs={{0,4},{4,8},{8,12},{12,16},{16,20},{20,24},{24,28},{28,0},{1,5},{5... | collective-permute-start | bytes 552968 | tf_op jit(solution)/shard_map/ppermute | solution.py:25
  20.8 10.2 %collective-permute-start.3 = (f32[3,20,6,128]{3,1,2,0:T(8,128)S(1)}, f32[3,20,6,128]{3,1,2,0:T(8,128)S(1)}, u32[]{:S(2)}, u32[]{:S(2)}) collective-permute-start(f32[3,20,6,128]{3,1,2,0:T(8,128)S(1)} %copy.133), channel_id=1, source_target_pairs={{4,0},{8,4},{12,8},{16,12},{20,16},{24,20},{28,24},{0,28},{5,1},{9... | collective-permute-start | bytes 552968 | tf_op jit(solution)/shard_map/ppermute | solution.py:28
  41.9 2.2 copy-start.1
  44.1 11.2 %collective-permute-start.4 = (f32[3,20,20,6]{2,1,3,0:T(8,128)S(1)}, f32[3,20,20,6]{2,1,3,0:T(8,128)S(1)}, u32[]{:S(2)}, u32[]{:S(2)}) collective-permute-start(f32[3,20,20,6]{2,1,3,0:T(8,128)S(1)} %get-tuple-element.24), channel_id=1, source_target_pairs={{0,1},{1,2},{2,3},{3,0},{4,5},{5,6},{6,7},{7,4},{8,9},{9,10},{10,1... | collective-permute-start | bytes 86408 | tf_op jit(solution)/shard_map/ppermute | solution.py:25
  46.1 9.8 %collective-permute-start.5 = (f32[3,20,20,6]{2,1,3,0:T(8,128)S(1)}, f32[3,20,20,6]{2,1,3,0:T(8,128)S(1)}, u32[]{:S(2)}, u32[]{:S(2)}) collective-permute-start(f32[3,20,20,6]{2,1,3,0:T(8,128)S(1)} %get-tuple-element.25), channel_id=1, source_target_pairs={{1,0},{2,1},{3,2},{0,3},{5,4},{6,5},{7,6},{4,7},{9,8},{10,9},{11,1... | collective-permute-start | bytes 86408 | tf_op jit(solution)/shard_map/ppermute | solution.py:28
  65.8 8.1 %collective-permute-start.6 = (f32[3,6,8,128]{3,2,1,0:T(8,128)S(1)}, f32[3,6,8,128]{3,2,1,0:T(8,128)S(1)}, u32[]{:S(2)}, u32[]{:S(2)}) collective-permute-start(f32[3,6,8,128]{3,2,1,0:T(8,128)S(1)} %get-tuple-element.110), channel_id=1, source_target_pairs={{0,32},{32,64},{64,96},{96,128},{128,160},{160,192},{192,224},{224... | collective-permute-start | bytes 221192 | tf_op jit(solution)/shard_map/ppermute | solution.py:25
  67.7 7.3 %collective-permute-start.7 = (f32[3,6,8,128]{3,2,1,0:T(8,128)S(1)}, f32[3,6,8,128]{3,2,1,0:T(8,128)S(1)}, u32[]{:S(2)}, u32[]{:S(2)}) collective-permute-start(f32[3,6,8,128]{3,2,1,0:T(8,128)S(1)} %get-tuple-element.111), channel_id=1, source_target_pairs={{32,0},{64,32},{96,64},{128,96},{160,128},{192,160},{224,192},{256... | collective-permute-start | bytes 221192 | tf_op jit(solution)/shard_map/ppermute | solution.py:28
  75.2 10.2 %collective-permute-start.8 = (f32[3,20,6,128]{3,1,2,0:T(8,128)S(1)}, f32[3,20,6,128]{3,1,2,0:T(8,128)S(1)}, u32[]{:S(2)}, u32[]{:S(2)}) collective-permute-start(f32[3,20,6,128]{3,1,2,0:T(8,128)S(1)} %copy.134), channel_id=1, source_target_pairs={{0,4},{4,8},{8,12},{12,16},{16,20},{20,24},{24,28},{28,0},{1,5},{5... | collective-permute-start | bytes 552968 | tf_op jit(solution)/shard_map/ppermute | solution.py:25
  79.6 10.2 %collective-permute-start.9 = (f32[3,20,6,128]{3,1,2,0:T(8,128)S(1)}, f32[3,20,6,128]{3,1,2,0:T(8,128)S(1)}, u32[]{:S(2)}, u32[]{:S(2)}) collective-permute-start(f32[3,20,6,128]{3,1,2,0:T(8,128)S(1)} %copy.135), channel_id=1, source_target_pairs={{4,0},{8,4},{12,8},{16,12},{20,16},{24,20},{28,24},{0,28},{5,1},{9... | collective-permute-start | bytes 552968 | tf_op jit(solution)/shard_map/ppermute | solution.py:28
  100.7 2.2 copy-start.2
  102.9 10.8 %collective-permute-start.10 = (f32[3,20,20,6]{2,1,3,0:T(8,128)S(1)}, f32[3,20,20,6]{2,1,3,0:T(8,128)S(1)}, u32[]{:S(2)}, u32[]{:S(2)}) collective-permute-start(f32[3,20,20,6]{2,1,3,0:T(8,128)S(1)} %get-tuple-element.22), channel_id=1, source_target_pairs={{0,1},{1,2},{2,3},{3,0},{4,5},{5,6},{6,7},{7,4},{8,9},{9,10},{10,1... | collective-permute-start | bytes 86408 | tf_op jit(solution)/shard_map/ppermute | solution.py:25
  104.8 9.3 %collective-permute-start.11 = (f32[3,20,20,6]{2,1,3,0:T(8,128)S(1)}, f32[3,20,20,6]{2,1,3,0:T(8,128)S(1)}, u32[]{:S(2)}, u32[]{:S(2)}) collective-permute-start(f32[3,20,20,6]{2,1,3,0:T(8,128)S(1)} %get-tuple-element.23), channel_id=1, source_target_pairs={{1,0},{2,1},{3,2},{0,3},{5,4},{6,5},{7,6},{4,7},{9,8},{10,9},{11,1... | collective-permute-start | bytes 86408 | tf_op jit(solution)/shard_map/ppermute | solution.py:28
  124.1 7.9 %collective-permute-start.12 = (f32[3,6,8,128]{3,2,1,0:T(8,128)S(1)}, f32[3,6,8,128]{3,2,1,0:T(8,128)S(1)}, u32[]{:S(2)}, u32[]{:S(2)}) collective-permute-start(f32[3,6,8,128]{3,2,1,0:T(8,128)S(1)} %get-tuple-element.108), channel_id=1, source_target_pairs={{0,32},{32,64},{64,96},{96,128},{128,160},{160,192},{192,224},{224... | collective-permute-start | bytes 221192 | tf_op jit(solution)/shard_map/ppermute | solution.py:25
  126.0 7.6 %collective-permute-start.13 = (f32[3,6,8,128]{3,2,1,0:T(8,128)S(1)}, f32[3,6,8,128]{3,2,1,0:T(8,128)S(1)}, u32[]{:S(2)}, u32[]{:S(2)}) collective-permute-start(f32[3,6,8,128]{3,2,1,0:T(8,128)S(1)} %get-tuple-element.109), channel_id=1, source_target_pairs={{32,0},{64,32},{96,64},{128,96},{160,128},{192,160},{224,192},{256... | collective-permute-start | bytes 221192 | tf_op jit(solution)/shard_map/ppermute | solution.py:28
  133.7 10.2 %collective-permute-start.14 = (f32[3,20,6,128]{3,1,2,0:T(8,128)S(1)}, f32[3,20,6,128]{3,1,2,0:T(8,128)S(1)}, u32[]{:S(2)}, u32[]{:S(2)}) collective-permute-start(f32[3,20,6,128]{3,1,2,0:T(8,128)S(1)} %copy.136), channel_id=1, source_target_pairs={{0,4},{4,8},{8,12},{12,16},{16,20},{20,24},{24,28},{28,0},{1,5},{5... | collective-permute-start | bytes 552968 | tf_op jit(solution)/shard_map/ppermute | solution.py:25
  138.0 11.3 %collective-permute-start.15 = (f32[3,20,6,128]{3,1,2,0:T(8,128)S(1)}, f32[3,20,6,128]{3,1,2,0:T(8,128)S(1)}, u32[]{:S(2)}, u32[]{:S(2)}) collective-permute-start(f32[3,20,6,128]{3,1,2,0:T(8,128)S(1)} %copy.137), channel_id=1, source_target_pairs={{4,0},{8,4},{12,8},{16,12},{20,16},{24,20},{28,24},{0,28},{5,1},{9... | collective-permute-start | bytes 552968 | tf_op jit(solution)/shard_map/ppermute | solution.py:28
  160.3 2.2 copy-start.3
  162.5 10.8 %collective-permute-start.16 = (f32[3,20,20,6]{2,1,3,0:T(8,128)S(1)}, f32[3,20,20,6]{2,1,3,0:T(8,128)S(1)}, u32[]{:S(2)}, u32[]{:S(2)}) collective-permute-start(f32[3,20,20,6]{2,1,3,0:T(8,128)S(1)} %get-tuple-element.20), channel_id=1, source_target_pairs={{0,1},{1,2},{2,3},{3,0},{4,5},{5,6},{6,7},{7,4},{8,9},{9,10},{10,1... | collective-permute-start | bytes 86408 | tf_op jit(solution)/shard_map/ppermute | solution.py:25
  164.6 9.2 %collective-permute-start.17 = (f32[3,20,20,6]{2,1,3,0:T(8,128)S(1)}, f32[3,20,20,6]{2,1,3,0:T(8,128)S(1)}, u32[]{:S(2)}, u32[]{:S(2)}) collective-permute-start(f32[3,20,20,6]{2,1,3,0:T(8,128)S(1)} %get-tuple-element.21), channel_id=1, source_target_pairs={{1,0},{2,1},{3,2},{0,3},{5,4},{6,5},{7,6},{4,7},{9,8},{10,9},{11,1... | collective-permute-start | bytes 86408 | tf_op jit(solution)/shard_map/ppermute | solution.py:28
  183.7 7.6 %collective-permute-start.18 = (f32[3,6,8,128]{3,2,1,0:T(8,128)S(1)}, f32[3,6,8,128]{3,2,1,0:T(8,128)S(1)}, u32[]{:S(2)}, u32[]{:S(2)}) collective-permute-start(f32[3,6,8,128]{3,2,1,0:T(8,128)S(1)} %get-tuple-element.106), channel_id=1, source_target_pairs={{0,32},{32,64},{64,96},{96,128},{128,160},{160,192},{192,224},{224... | collective-permute-start | bytes 221192 | tf_op jit(solution)/shard_map/ppermute | solution.py:25
  185.7 7.2 %collective-permute-start.19 = (f32[3,6,8,128]{3,2,1,0:T(8,128)S(1)}, f32[3,6,8,128]{3,2,1,0:T(8,128)S(1)}, u32[]{:S(2)}, u32[]{:S(2)}) collective-permute-start(f32[3,6,8,128]{3,2,1,0:T(8,128)S(1)} %get-tuple-element.107), channel_id=1, source_target_pairs={{32,0},{64,32},{96,64},{128,96},{160,128},{192,160},{224,192},{256... | collective-permute-start | bytes 221192 | tf_op jit(solution)/shard_map/ppermute | solution.py:28
  193.0 12.3 %collective-permute-start.20 = (f32[3,20,6,128]{3,1,2,0:T(8,128)S(1)}, f32[3,20,6,128]{3,1,2,0:T(8,128)S(1)}, u32[]{:S(2)}, u32[]{:S(2)}) collective-permute-start(f32[3,20,6,128]{3,1,2,0:T(8,128)S(1)} %copy.138), channel_id=1, source_target_pairs={{0,4},{4,8},{8,12},{12,16},{16,20},{20,24},{24,28},{28,0},{1,5},{5... | collective-permute-start | bytes 552968 | tf_op jit(solution)/shard_map/ppermute | solution.py:25
  197.9 10.7 %collective-permute-start.21 = (f32[3,20,6,128]{3,1,2,0:T(8,128)S(1)}, f32[3,20,6,128]{3,1,2,0:T(8,128)S(1)}, u32[]{:S(2)}, u32[]{:S(2)}) collective-permute-start(f32[3,20,6,128]{3,1,2,0:T(8,128)S(1)} %copy.139), channel_id=1, source_target_pairs={{4,0},{8,4},{12,8},{16,12},{20,16},{24,20},{28,24},{0,28},{5,1},{9... | collective-permute-start | bytes 552968 | tf_op jit(solution)/shard_map/ppermute | solution.py:28
  219.6 2.2 copy-start
  221.8 11.8 %collective-permute-start.22 = (f32[3,20,20,6]{2,1,3,0:T(8,128)S(1)}, f32[3,20,20,6]{2,1,3,0:T(8,128)S(1)}, u32[]{:S(2)}, u32[]{:S(2)}) collective-permute-start(f32[3,20,20,6]{2,1,3,0:T(8,128)S(1)} %get-tuple-element.18), channel_id=1, source_target_pairs={{0,1},{1,2},{2,3},{3,0},{4,5},{5,6},{6,7},{7,4},{8,9},{9,10},{10,1... | collective-permute-start | bytes 86408 | tf_op jit(solution)/shard_map/ppermute | solution.py:25
  223.7 10.3 %collective-permute-start.23 = (f32[3,20,20,6]{2,1,3,0:T(8,128)S(1)}, f32[3,20,20,6]{2,1,3,0:T(8,128)S(1)}, u32[]{:S(2)}, u32[]{:S(2)}) collective-permute-start(f32[3,20,20,6]{2,1,3,0:T(8,128)S(1)} %get-tuple-element.19), channel_id=1, source_target_pairs={{1,0},{2,1},{3,2},{0,3},{5,4},{6,5},{7,6},{4,7},{9,8},{10,9},{11,1... | collective-permute-start | bytes 86408 | tf_op jit(solution)/shard_map/ppermute | solution.py:28
  244.0 1.0 copy-start.5
  244.9 11.5 %copy-start.6 = (s32[512,128]{1,0:T(8,128)S(1)}, s32[512,128]{1,0:T(8,128)}, u32[]{:S(2)}) copy-start(s32[512,128]{1,0:T(8,128)} %param.7) | copy-start | bytes 786436
  245.0 11.5 %copy-start.7 = (s32[4]{0:T(128)S(1)}, s32[4]{0:T(128)}, u32[]{:S(2)}) copy-start(s32[4]{0:T(128)} %param.8) | copy-start | bytes 52
  246.5 22.7 %all-to-all-start = ((f32[16,1,384]{2,1,0:T(1,128)}), f32[16,1,384]{2,1,0:T(1,128)S(1)}, u32[]{:S(2)}, u32[]{:S(2)}) async-start(f32[16,1,384]{2,1,0:T(1,128)} %reshape.103), calls=%async_computation | async-start | bytes 49152 | tf_op jit(solution)/shard_map/all_to_all | solution.py:115
  256.4 16.2 %copy-start.4 = (f32[3,8,1,2,32,128]{5,4,3,2,1,0:T(8,128)S(1)}, f32[3,8,1,2,32,128]{5,4,3,2,1,0:T(8,128)}, u32[]{:S(2)}) copy-start(f32[3,8,1,2,32,128]{5,4,3,2,1,0:T(8,128)} %param.6) | copy-start | bytes 2359300
  274.9 3.1 collective-permute-start.24
  278.0 7.7 %collective-permute-start.25 = (f32[128,128]{0,1:T(8,128)S(1)}, f32[128,128]{0,1:T(8,128)S(1)}, u32[]{:S(2)}, u32[]{:S(2)}) collective-permute-start(f32[128,128]{0,1:T(8,128)S(1)} %add.1084), channel_id=1, source_target_pairs={{0,2},{1,3},{2,0},{3,1},{4,6},{5,7},{6,4},{7,5},{8,10},{9,11},{10,... | collective-permute-start | bytes 196616 | tf_op jit(solution)/shard_map/ppermute | solution.py:99
  285.7 8.0 %collective-permute-start.26 = (f32[128,128]{0,1:T(8,128)S(1)}, f32[128,128]{0,1:T(8,128)S(1)}, u32[]{:S(2)}, u32[]{:S(2)}) collective-permute-start(f32[128,128]{0,1:T(8,128)S(1)} %add.1085), channel_id=1, source_target_pairs={{0,4},{4,0},{8,12},{12,8},{16,20},{20,16},{24,28},{28,24},{1,5},{5... | collective-permute-start | bytes 196616 | tf_op jit(solution)/shard_map/ppermute | solution.py:99
  293.7 6.2 %collective-permute-start.27 = (f32[128,128]{0,1:T(8,128)S(1)}, f32[128,128]{0,1:T(8,128)S(1)}, u32[]{:S(2)}, u32[]{:S(2)}) collective-permute-start(f32[128,128]{0,1:T(8,128)S(1)} %add.1086), channel_id=1, source_target_pairs={{0,8},{4,12},{8,0},{12,4},{16,24},{20,28},{24,16},{28,20},{1,9},{5... | collective-permute-start | bytes 196616 | tf_op jit(solution)/shard_map/ppermute | solution.py:99
  299.9 7.7 %collective-permute-start.28 = (f32[128,128]{0,1:T(8,128)S(1)}, f32[128,128]{0,1:T(8,128)S(1)}, u32[]{:S(2)}, u32[]{:S(2)}) collective-permute-start(f32[128,128]{0,1:T(8,128)S(1)} %add.1087), channel_id=1, source_target_pairs={{0,16},{4,20},{8,24},{12,28},{16,0},{20,4},{24,8},{28,12},{1,17},{... | collective-permute-start | bytes 196616 | tf_op jit(solution)/shard_map/ppermute | solution.py:99
  307.6 6.2 %collective-permute-start.29 = (f32[128,128]{0,1:T(8,128)S(1)}, f32[128,128]{0,1:T(8,128)S(1)}, u32[]{:S(2)}, u32[]{:S(2)}) collective-permute-start(f32[128,128]{0,1:T(8,128)S(1)} %add.1088), channel_id=1, source_target_pairs={{0,32},{32,0},{64,96},{96,64},{128,160},{160,128},{192,224},{224,1... | collective-permute-start | bytes 196616 | tf_op jit(solution)/shard_map/ppermute | solution.py:99
  313.8 7.1 %collective-permute-start.30 = (f32[128,128]{0,1:T(8,128)S(1)}, f32[128,128]{0,1:T(8,128)S(1)}, u32[]{:S(2)}, u32[]{:S(2)}) collective-permute-start(f32[128,128]{0,1:T(8,128)S(1)} %add.1089), channel_id=1, source_target_pairs={{0,64},{32,96},{64,0},{96,32},{128,192},{160,224},{192,128},{224,1... | collective-permute-start | bytes 196616 | tf_op jit(solution)/shard_map/ppermute | solution.py:99
  320.8 11.6 %collective-permute-start.31 = (f32[128,128]{0,1:T(8,128)S(1)}, f32[128,128]{0,1:T(8,128)S(1)}, u32[]{:S(2)}, u32[]{:S(2)}) collective-permute-start(f32[128,128]{0,1:T(8,128)S(1)} %add.1090), channel_id=1, source_target_pairs={{0,128},{32,160},{64,192},{96,224},{128,0},{160,32},{192,64},{224,... | collective-permute-start | bytes 196616 | tf_op jit(solution)/shard_map/ppermute | solution.py:99
  332.4 15.4 %collective-permute-start.32 = (f32[128,128]{0,1:T(8,128)S(1)}, f32[128,128]{0,1:T(8,128)S(1)}, u32[]{:S(2)}, u32[]{:S(2)}) collective-permute-start(f32[128,128]{0,1:T(8,128)S(1)} %add.1091), channel_id=1, source_target_pairs={{0,256},{32,288},{64,320},{96,352},{128,384},{160,416},{192,448},{... | collective-permute-start | bytes 196616 | tf_op jit(solution)/shard_map/ppermute | solution.py:99
